TPU v7x, 256 devices: a whole 4x4x8 slice. The times are simulated.
256 devices in a mesh: row: 16 (over z, core), col: 16 (over y, x).
Axes of the slice: x: 4, y: 4, z: 8, core: 2. Of those that a mesh axis runs over, the one named last changes fastest.
Arguments:
- prior_window_motion: float32 [3, 128, 128, 256], P(None, 'row', 'col'), may hold values from -1.2 to 1.2
- prior_window_stress: float32 [128, 128, 256], P('row', 'col'), may hold values from -3 to 3
- heat_scalar: float32 [128, 128, 256], P('row', 'col'), may hold values from 0 to 1
Outputs:
- velocity: float32 [3, 128, 128, 256], P(None, 'row', 'col')
- pressure: float32 [128, 128, 256], P('row', 'col')
All inputs are finite; a program needn't handle non-finite values.
Results may differ from a plain program's by a relative error of at most 0.0003.
Values sent between devices are 32-bit elements; how exact they have to be, the bound alone decides.
No kernel may reach another device: no remote copies, remote signals or barrier semaphores. Data moves between devices by JAX's collectives and lax.ppermute only.
A program may use at most 64 MiB of HBM per device.

v0:
```python
import jax
import jax.numpy as jnp
from jax import lax
from jax.sharding import PartitionSpec as P

OUTER = 2
INNER = 2
PRECISE = lax.Precision.HIGHEST
ENABLE_SWITCH = 2.0
OFFSET_COUNT = 0.5
AUGMENT = 1.0
ANCHOR = 0.002
RAYLEIGH_NUMBER = 1.0
SMOOTHING = 2.0


def padded(cells, sides, width):
    for axis, dim in sides:
        count = lax.axis_size(axis)
        head = lax.slice_in_dim(cells, 0, width, axis=dim)
        tail = lax.slice_in_dim(cells, cells.shape[dim] - width, cells.shape[dim], axis=dim)
        cells = jnp.concatenate(
            [
                lax.ppermute(tail, axis, [(i, (i + 1) % count) for i in range(count)]),
                cells,
                lax.ppermute(head, axis, [((i + 1) % count, i) for i in range(count)]),
            ],
            axis=dim,
        )
    return cells


def global_sum(value):
    count = lax.axis_size("row") * lax.axis_size("col")
    spread = jnp.broadcast_to(value.reshape(1), (count,))
    gathered = lax.all_to_all(spread, ("row", "col"), 0, 0, tiled=True)
    return jnp.sum(gathered)


def from_behind(value, axis, steps):
    count = lax.axis_size(axis)
    pairs = [(source, (source + steps) % count) for source in range(count)]
    return lax.ppermute(value, axis, pairs)


def cas_matrix(extent):
    index = jnp.arange(extent, dtype=jnp.int32)
    phase = index[:, None] * index[None, :] % extent
    angle = 2.0 * jnp.pi / extent * phase.astype(jnp.float32)
    return jnp.cos(angle) + jnp.sin(angle)


def eigen_row(number, offset_index, extent):
    index = offset_index + jnp.arange(number, dtype=jnp.int32)
    return 2.0 - 2.0 * jnp.cos(2.0 * jnp.pi / extent * index.astype(jnp.float32))


def precondition(residual, tables):
    xtable, ytable, ztable = tables
    row_count = lax.axis_size("row")
    col_count = lax.axis_size("col")
    components, owned_height_lines, owned_depth_slices, period_extent_first = residual.shape
    ylength = owned_height_lines * row_count
    zlength = owned_depth_slices * col_count
    normal_factor = 1.0 / (period_extent_first * ylength * zlength)
    xpiece = period_extent_first // row_count
    ypiece = ylength // col_count
    spectrum = jnp.einsum("kx,cyzx->cykz", xtable, residual, precision=PRECISE).reshape(
        components, owned_height_lines, period_extent_first * owned_depth_slices
    )
    spectrum = lax.all_to_all(spectrum, "row", split_axis=2, concat_axis=1, tiled=True)
    spectrum = jnp.einsum(
        "ky,cyxz->czkx",
        ytable,
        spectrum.reshape(components, ylength, xpiece, owned_depth_slices),
        precision=PRECISE,
    ).reshape(components, owned_depth_slices, ylength * xpiece)
    spectrum = lax.all_to_all(spectrum, "col", split_axis=2, concat_axis=1, tiled=True)
    zeigen = eigen_row(zlength, 0, zlength)
    yeigen = eigen_row(ypiece, lax.axis_index("col") * ypiece, ylength)
    xeigen = eigen_row(xpiece, lax.axis_index("row") * xpiece, period_extent_first)
    mixed_eigen = (yeigen[:, None] + xeigen[None, :]).reshape(-1)
    symbol = normal_factor / (SMOOTHING * (zeigen[:, None] + mixed_eigen[None, :]) + ANCHOR)
    spectrum = jnp.einsum("kz,czm->ckm", ztable, spectrum, precision=PRECISE)
    spectrum = jnp.einsum("kz,czm->ckm", ztable, spectrum * symbol[None], precision=PRECISE)
    spectrum = lax.all_to_all(spectrum, "col", split_axis=1, concat_axis=2, tiled=True)
    spectrum = jnp.einsum(
        "ky,czyx->ckxz",
        ytable,
        spectrum.reshape(components, owned_depth_slices, ylength, xpiece),
        precision=PRECISE,
    ).reshape(components, ylength, xpiece * owned_depth_slices)
    spectrum = lax.all_to_all(spectrum, "row", split_axis=1, concat_axis=2, tiled=True)
    return jnp.einsum(
        "kx,cyxz->cyzk",
        xtable,
        spectrum.reshape(components, owned_height_lines, period_extent_first, owned_depth_slices),
        precision=PRECISE,
    )


def forward(extended, direction):
    owned_height_lines = extended.shape[-3] - 2
    owned_depth_slices = extended.shape[-2] - 2
    root = extended[..., : owned_height_lines + 1, : owned_depth_slices + 1, :]
    if direction == 0:
        return jnp.roll(root, -1, -1) - root
    if direction == 1:
        return extended[..., 1 : owned_height_lines + 2, : owned_depth_slices + 1, :] - root
    return extended[..., : owned_height_lines + 1, 1 : owned_depth_slices + 2, :] - root


def backward(region, direction):
    center = region[..., 1:, 1:, :]
    if direction == 0:
        return center - jnp.roll(center, 1, -1)
    if direction == 1:
        return center - region[..., :-1, 1:, :]
    return center - region[..., 1:, :-1, :]


def extend(field):
    return padded(field, (("row", 1), ("col", 2)), 1)


def lower_region(pressure):
    below_y = from_behind(pressure[-1:], "row", 1)
    below_z = from_behind(pressure[:, -1:], "col", 1)
    corner = jnp.zeros((1, 1, pressure.shape[2]), jnp.float32)
    upper_band = jnp.concatenate([corner, below_y], 1)
    main_band = jnp.concatenate([below_z, pressure], 1)
    return jnp.concatenate([upper_band, main_band], 0)


def operate(extended, shear_resistance_map):
    owned_height_lines = extended.shape[1] - 2
    owned_depth_slices = extended.shape[2] - 2
    gradients = [[forward(extended[target], source) for source in range(3)] for target in range(3)]
    spread = gradients[0][0] + gradients[1][1] + gradients[2][2]
    result = []
    for target in range(3):
        summed = (
            ANCHOR * extended[target, 1 : owned_height_lines + 1, 1 : owned_depth_slices + 1, :]
        )
        for source in range(3):
            fluxes = shear_resistance_map * (gradients[target][source] + gradients[source][target])
            if target == source:
                fluxes = fluxes + AUGMENT * spread
            summed = summed - backward(fluxes, source)
        result.append(summed)
    return jnp.stack(result)


def pressure_gradient(region):
    return jnp.stack([-backward(region, target) for target in range(3)])


def divergence_region(extended):
    return forward(extended[0], 0) + forward(extended[1], 1) + forward(extended[2], 2)


def per_device(prior_window_motion, prior_window_stress, heat_scalar):
    owned_height_lines, owned_depth_slices, period_extent_first = heat_scalar.shape
    tables = (
        cas_matrix(period_extent_first),
        cas_matrix(owned_height_lines * lax.axis_size("row")),
        cas_matrix(owned_depth_slices * lax.axis_size("col")),
    )
    stacked_fields = jnp.concatenate(
        [prior_window_motion, prior_window_stress[None], heat_scalar[None]], 0
    )
    extended = padded(stacked_fields, (("row", 1), ("col", 2)), 1)
    shear_resistance_map = jnp.exp(
        ENABLE_SWITCH
        * (
            1.0
            / (extended[4, : owned_height_lines + 1, : owned_depth_slices + 1, :] + OFFSET_COUNT)
            - 1.0 / (0.5 + OFFSET_COUNT)
        )
    )
    thermal_lift = RAYLEIGH_NUMBER * (heat_scalar - 0.5)
    zeroes = jnp.zeros_like(thermal_lift)
    forcing = jnp.stack([zeroes, zeroes, thermal_lift])
    velocity = prior_window_motion
    pressure = prior_window_stress
    velocity_ext = extended[0:3]
    pushing = pressure_gradient(extended[3, : owned_height_lines + 1, : owned_depth_slices + 1, :])
    spread_now = jnp.zeros_like(shear_resistance_map)
    for outer_step in range(OUTER):
        if outer_step > 0:
            pushing = pressure_gradient(lower_region(pressure))
        residual = forcing - pushing - operate(velocity_ext, shear_resistance_map)
        direction = residual
        image = residual
        energy_now = jnp.float32(1.0)
        step_size = jnp.float32(1.0)
        for inner_step in range(INNER):
            precond = precondition(residual, tables)
            energy_next = global_sum(jnp.sum(residual * precond))
            if inner_step == 0:
                direction = precond
            else:
                direction = precond + energy_next / energy_now * direction
            energy_now = energy_next
            image = operate(extend(direction), shear_resistance_map)
            curvature = global_sum(jnp.sum(direction * image))
            step_size = energy_now / curvature
            velocity = velocity + step_size * direction
            residual = residual - step_size * image
        velocity_ext = extend(velocity)
        spread_now = divergence_region(velocity_ext)
        pressure = pressure + AUGMENT * spread_now[1:, 1:, :]
    return (velocity, pressure)


def solution(mesh):
    placed = (P(None, "row", "col", None), P("row", "col", None), P("row", "col", None))
    return jax.shard_map(
        per_device,
        mesh=mesh,
        in_specs=placed,
        out_specs=(P(None, "row", "col", None), P("row", "col", None)),
        check_vma=False,
    )
```

profile of v0, /device:TPU:30, one launch (start us, length us, event | category | flops | bytes accessed | tf_op | source)
XLA Modules:
  0.0 742.4 jit_solution(7646809558216230969)
XLA Ops:
  97.4 12.2 %all_to_all.300 = f32[3,128,128]{2,0,1:T(4,128)S(1)} all-to-all(f32[3,128,128]{2,0,1:T(4,128)S(1)} %copy.371), channel_id=1, replica_groups=mesh['row'=16,'col'=16] {'col'}, dimensions={1} | all-to-all | bytes 393216 | tf_op jit(solution)/shard_map/all_to_all | solution.py:86
  112.9 13.7 %all_to_all.301 = f32[3,128,128]{2,0,1:T(4,128)S(1)} all-to-all(f32[3,128,128]{2,0,1:T(4,128)S(1)} %copy.376), channel_id=1, replica_groups=mesh['row'=16,'col'=16] {'row'}, dimensions={1} | all-to-all | bytes 393216 | tf_op jit(solution)/shard_map/all_to_all | solution.py:93
  154.3 18.4 %all_to_all.302 = f32[256,1,1]{2,1,0:T(1,128)S(1)} all-to-all(f32[256,1,1]{2,1,0:T(1,128)S(1)} %broadcast_in_dim.23), channel_id=1, replica_groups=mesh['row'=16,'col'=16] {'row','col'}, dimensions={0} | all-to-all | bytes 2048 | tf_op jit(solution)/shard_map/all_to_all | solution.py:36
  174.1 9.1 %all-to-all-start.4 = ((f32[256,1,1]{2,1,0:T(1,128)}), f32[256,1,1]{2,1,0:T(1,128)S(1)}, u32[]{:S(2)}, u32[]{:S(2)}) async-start(f32[256,1,1]{2,1,0:T(1,128)} %broadcast_in_dim.22), calls=%async_computation.4 | async-start | bytes 262144 | tf_op jit(solution)/shard_map/all_to_all | solution.py:36
  184.2 8.8 %all-to-all-done.4 = f32[256,1,1]{2,1,0:T(1,128)S(1)} async-done(((f32[256,1,1]{2,1,0:T(1,128)}), f32[256,1,1]{2,1,0:T(1,128)S(1)}, u32[]{:S(2)}, u32[]{:S(2)}) %all-to-all-start.4) | async-done | bytes 1056 | tf_op jit(solution)/shard_map/all_to_all | solution.py:36
  205.6 12.5 %all_to_all.303 = f32[16,1,3072]{2,1,0:T(1,128)S(1)} all-to-all(f32[16,1,3072]{2,1,0:T(1,128)S(1)} %reshape.266), channel_id=1, replica_groups=mesh['row'=16,'col'=16] {'row'}, dimensions={0} | all-to-all | bytes 393216 | tf_op jit(solution)/shard_map/all_to_all | solution.py:71
  245.0 11.3 %all_to_all.304 = f32[16,1,3072]{2,1,0:T(1,128)S(1)} all-to-all(f32[16,1,3072]{2,1,0:T(1,128)S(1)} %reshape.268), channel_id=1, replica_groups=mesh['row'=16,'col'=16] {'col'}, dimensions={0} | all-to-all | bytes 393216 | tf_op jit(solution)/shard_map/all_to_all | solution.py:78
  266.2 12.1 %all_to_all.305 = f32[3,128,128]{2,0,1:T(4,128)S(1)} all-to-all(f32[3,128,128]{2,0,1:T(4,128)S(1)} %copy.392), channel_id=1, replica_groups=mesh['row'=16,'col'=16] {'col'}, dimensions={1} | all-to-all | bytes 393216 | tf_op jit(solution)/shard_map/all_to_all | solution.py:86
  281.6 13.6 %all_to_all.306 = f32[3,128,128]{2,0,1:T(4,128)S(1)} all-to-all(f32[3,128,128]{2,0,1:T(4,128)S(1)} %copy.397), channel_id=1, replica_groups=mesh['row'=16,'col'=16] {'row'}, dimensions={1} | all-to-all | bytes 393216 | tf_op jit(solution)/shard_map/all_to_all | solution.py:93
  307.4 18.9 %all_to_all.307 = f32[256,1,1]{2,1,0:T(1,128)S(1)} all-to-all(f32[256,1,1]{2,1,0:T(1,128)S(1)} %broadcast_in_dim.24), channel_id=1, replica_groups=mesh['row'=16,'col'=16] {'row','col'}, dimensions={0} | all-to-all | bytes 2048 | tf_op jit(solution)/shard_map/all_to_all | solution.py:36
  347.7 17.9 %all_to_all.308 = f32[256,1,1]{2,1,0:T(1,128)S(1)} all-to-all(f32[256,1,1]{2,1,0:T(1,128)S(1)} %broadcast_in_dim.25), channel_id=1, replica_groups=mesh['row'=16,'col'=16] {'row','col'}, dimensions={0} | all-to-all | bytes 2048 | tf_op jit(solution)/shard_map/all_to_all | solution.py:36
  400.0 12.6 %all_to_all.309 = f32[16,1,3072]{2,1,0:T(1,128)S(1)} all-to-all(f32[16,1,3072]{2,1,0:T(1,128)S(1)} %reshape.270), channel_id=1, replica_groups=mesh['row'=16,'col'=16] {'row'}, dimensions={0} | all-to-all | bytes 393216 | tf_op jit(solution)/shard_map/all_to_all | solution.py:71
  435.7 11.4 %all_to_all.310 = f32[16,1,3072]{2,1,0:T(1,128)S(1)} all-to-all(f32[16,1,3072]{2,1,0:T(1,128)S(1)} %reshape.272), channel_id=1, replica_groups=mesh['row'=16,'col'=16] {'col'}, dimensions={0} | all-to-all | bytes 393216 | tf_op jit(solution)/shard_map/all_to_all | solution.py:78
  457.0 12.2 %all_to_all.311 = f32[3,128,128]{2,0,1:T(4,128)S(1)} all-to-all(f32[3,128,128]{2,0,1:T(4,128)S(1)} %copy.413), channel_id=1, replica_groups=mesh['row'=16,'col'=16] {'col'}, dimensions={1} | all-to-all | bytes 393216 | tf_op jit(solution)/shard_map/all_to_all | solution.py:86
  472.5 13.6 %all_to_all.312 = f32[3,128,128]{2,0,1:T(4,128)S(1)} all-to-all(f32[3,128,128]{2,0,1:T(4,128)S(1)} %copy.418), channel_id=1, replica_groups=mesh['row'=16,'col'=16] {'row'}, dimensions={1} | all-to-all | bytes 393216 | tf_op jit(solution)/shard_map/all_to_all | solution.py:93
  512.3 18.5 %all_to_all.313 = f32[256,1,1]{2,1,0:T(1,128)S(1)} all-to-all(f32[256,1,1]{2,1,0:T(1,128)S(1)} %broadcast_in_dim.27), channel_id=1, replica_groups=mesh['row'=16,'col'=16] {'row','col'}, dimensions={0} | all-to-all | bytes 2048 | tf_op jit(solution)/shard_map/all_to_all | solution.py:36
  532.2 9.1 %all-to-all-start.16 = ((f32[256,1,1]{2,1,0:T(1,128)}), f32[256,1,1]{2,1,0:T(1,128)S(1)}, u32[]{:S(2)}, u32[]{:S(2)}) async-start(f32[256,1,1]{2,1,0:T(1,128)} %broadcast_in_dim.26), calls=%async_computation.16 | async-start | bytes 262144 | tf_op jit(solution)/shard_map/all_to_all | solution.py:36
  542.2 8.9 %all-to-all-done.16 = f32[256,1,1]{2,1,0:T(1,128)S(1)} async-done(((f32[256,1,1]{2,1,0:T(1,128)}), f32[256,1,1]{2,1,0:T(1,128)S(1)}, u32[]{:S(2)}, u32[]{:S(2)}) %all-to-all-start.16) | async-done | bytes 1056 | tf_op jit(solution)/shard_map/all_to_all | solution.py:36
  563.6 12.5 %all_to_all.314 = f32[16,1,3072]{2,1,0:T(1,128)S(1)} all-to-all(f32[16,1,3072]{2,1,0:T(1,128)S(1)} %reshape.274), channel_id=1, replica_groups=mesh['row'=16,'col'=16] {'row'}, dimensions={0} | all-to-all | bytes 393216 | tf_op jit(solution)/shard_map/all_to_all | solution.py:71
  602.9 11.3 %all_to_all.315 = f32[16,1,3072]{2,1,0:T(1,128)S(1)} all-to-all(f32[16,1,3072]{2,1,0:T(1,128)S(1)} %reshape.276), channel_id=1, replica_groups=mesh['row'=16,'col'=16] {'col'}, dimensions={0} | all-to-all | bytes 393216 | tf_op jit(solution)/shard_map/all_to_all | solution.py:78
  624.1 11.9 %all_to_all.316 = f32[3,128,128]{2,0,1:T(4,128)S(1)} all-to-all(f32[3,128,128]{2,0,1:T(4,128)S(1)} %copy.434), channel_id=1, replica_groups=mesh['row'=16,'col'=16] {'col'}, dimensions={1} | all-to-all | bytes 393216 | tf_op jit(solution)/shard_map/all_to_all | solution.py:86
  639.4 13.6 %all_to_all.317 = f32[3,128,128]{2,0,1:T(4,128)S(1)} all-to-all(f32[3,128,128]{2,0,1:T(4,128)S(1)} %copy.439), channel_id=1, replica_groups=mesh['row'=16,'col'=16] {'row'}, dimensions={1} | all-to-all | bytes 393216 | tf_op jit(solution)/shard_map/all_to_all | solution.py:93
  665.0 18.9 %all_to_all.318 = f32[256,1,1]{2,1,0:T(1,128)S(1)} all-to-all(f32[256,1,1]{2,1,0:T(1,128)S(1)} %broadcast_in_dim.28), channel_id=1, replica_groups=mesh['row'=16,'col'=16] {'row','col'}, dimensions={0} | all-to-all | bytes 2048 | tf_op jit(solution)/shard_map/all_to_all | solution.py:36
  705.2 17.9 %all_to_all.319 = f32[256,1,1]{2,1,0:T(1,128)S(1)} all-to-all(f32[256,1,1]{2,1,0:T(1,128)S(1)} %broadcast_in_dim.29), channel_id=1, replica_groups=mesh['row'=16,'col'=16] {'row','col'}, dimensions={0} | all-to-all | bytes 2048 | tf_op jit(solution)/shard_map/all_to_all | solution.py:36
  (449 shorter events, 410.4 us)
Async XLA Ops:
  1.5 7.0 collective-permute-start
  1.6 7.0 collective-permute-start.1
  10.0 7.5 %collective-permute-start.3 = (f32[5,10,1,256]{3,2,1,0:T(1,128)S(1)}, f32[5,10,1,256]{3,2,1,0:T(1,128)S(1)}, u32[]{:S(2)}, u32[]{:S(2)}) collective-permute-start(f32[5,10,1,256]{3,2,1,0:T(1,128)S(1)} %get-tuple-element.50), channel_id=1, source_target_pairs={{1,0},{2,1},{3,2},{4,3},{5,4},{6,5},{7,6},{8,7},{9,8},{10,9},{11,1... | collective-permute-start | bytes 153608 | tf_op jit(solution)/shard_map/ppermute | solution.py:26
  31.7 16.3 %all-to-all-start = ((f32[16,1,3072]{2,1,0:T(1,128)}), f32[16,1,3072]{2,1,0:T(1,128)S(1)}, u32[]{:S(2)}, u32[]{:S(2)}) async-start(f32[16,1,3072]{2,1,0:T(1,128)} %reshape.262), calls=%async_computation | async-start | bytes 393216 | tf_op jit(solution)/shard_map/all_to_all | solution.py:71
  76.0 11.5 %all-to-all-start.1 = ((f32[16,1,3072]{2,1,0:T(1,128)}), f32[16,1,3072]{2,1,0:T(1,128)S(1)}, u32[]{:S(2)}, u32[]{:S(2)}) async-start(f32[16,1,3072]{2,1,0:T(1,128)} %reshape.264), calls=%async_computation.1 | async-start | bytes 393216 | tf_op jit(solution)/shard_map/all_to_all | solution.py:78
  135.6 4.5 collective-permute-start.4
  140.1 5.7 collective-permute-start.6
  144.3 7.2 collective-permute-start.7
  174.1 18.9 %all-to-all-start.4 = ((f32[256,1,1]{2,1,0:T(1,128)}), f32[256,1,1]{2,1,0:T(1,128)S(1)}, u32[]{:S(2)}, u32[]{:S(2)}) async-start(f32[256,1,1]{2,1,0:T(1,128)} %broadcast_in_dim.22), calls=%async_computation.4 | async-start | bytes 262144 | tf_op jit(solution)/shard_map/all_to_all | solution.py:36
  329.5 4.5 collective-permute-start.8
  334.1 5.3 collective-permute-start.10
  337.8 7.2 collective-permute-start.11
  367.8 4.5 collective-permute-start.12
  372.4 5.3 collective-permute-start.14
  376.1 7.2 collective-permute-start.15
  493.5 4.5 collective-permute-start.18
  498.0 5.7 collective-permute-start.20
  502.1 7.2 collective-permute-start.21
  532.2 18.9 %all-to-all-start.16 = ((f32[256,1,1]{2,1,0:T(1,128)}), f32[256,1,1]{2,1,0:T(1,128)S(1)}, u32[]{:S(2)}, u32[]{:S(2)}) async-start(f32[256,1,1]{2,1,0:T(1,128)} %broadcast_in_dim.26), calls=%async_computation.16 | async-start | bytes 262144 | tf_op jit(solution)/shard_map/all_to_all | solution.py:36
  687.1 4.5 collective-permute-start.22
  691.6 5.3 collective-permute-start.24
  695.4 7.2 collective-permute-start.25
  729.9 5.3 collective-permute-start.28
  733.7 7.2 collective-permute-start.29
  (64 other events, 830.4 us)
where the time goes:
time: 750 us; the launch traced here: 742 us
  blocking collectives  285 us (38%)
  local copies, waits for them, and re-layouts  171 us (23%)
  waiting for transfers between devices  92.7 us (12%)
  starting transfers between devices  80.1 us (11%)
  matrix products  71.2 us (9%)
  other arithmetic  31.2 us (4%)
  between operations  11 us (1%)
    all_to_all x6, blocking collectives, global_sum(): gathered = lax.all_to_all(spread, ('row', 'col'), 0, 0, tiled=True)  110 us
    unnamed x124, local copies, waits for them, and re-layouts  70.6 us
    all_to_all x4, blocking collectives, precondition(): lax.all_to_all(spectrum, 'row', split_axis=1, concat_axis=2, tiled=True)  54.6 us
    all_to_all x4, blocking collectives, precondition(): lax.all_to_all(spectrum, 'col', split_axis=1, concat_axis=2, tiled=True)  48.3 us
    all_to_all x3, blocking collectives, precondition(): lax.all_to_all(spectrum, 'row', split_axis=2, concat_axis=1, tiled=True)  37.7 us
    ppermute x14, waiting for transfers between devices, padded(): lax.ppermute(head, axis, [((i + 1) % count, i) for i in range(count)])  36.5 us
    all_to_all x3, blocking collectives, precondition(): lax.all_to_all(spectrum, 'col', split_axis=2, concat_axis=1, tiled=True)  34 us
    dot_general x4, matrix products, precondition(): jnp.einsum('kx,cyxz->cyzk', xtable, spectrum.reshape(components, owned_he...  27.1 us
  transfers between devices with their start and end apart: 34, of which 26 were waited for; matrix products, arithmetic and copies ran while one was open for 1% of the time, Pallas kernels for 0%

commit v1 on v0

--- a/solution.py
+++ b/solution.py
@@ -68,7 +68,10 @@
     spectrum = jnp.einsum("kx,cyzx->cykz", xtable, residual, precision=PRECISE).reshape(
         components, owned_height_lines, period_extent_first * owned_depth_slices
     )
-    spectrum = lax.all_to_all(spectrum, "row", split_axis=2, concat_axis=1, tiled=True)
+    spectrum = jnp.concatenate(
+        lax.all_to_all(jnp.stack(jnp.split(spectrum, lax.axis_size("row"), axis=2)), "row", 0, 0),
+        axis=1,
+    )
     spectrum = jnp.einsum(
         "ky,cyxz->czkx",
         ytable,

time: 750 us -> 733 us (0.977)
  matrix products: 71.2 us -> 55.7 us
    another operation x0 -> x12, local copies, waits for them, and re-layouts: none -> 18 us  [the longest x8 15.2 us: precondition(): spectrum.reshape(components, ylength, xpiece, owned_depth_slices)]
    dot_general x4, matrix products: 22.9 us -> 5.1 us  [precondition(): jnp.einsum('ky,cyxz->czkx', ytable, spectrum.reshape(components, ylength,...]
    all_to_all x5 -> x0, local copies, waits for them, and re-layouts: 16.5 us -> none  [precondition(): lax.all_to_all(spectrum, 'row', split_axis=2, concat_axis=1, tiled=True)]
    reshape x4 -> x0, local copies, waits for them, and re-layouts: 9.64 us -> none  [precondition(): spectrum.reshape(components, ylength, xpiece, owned_depth_slices)]
    unnamed x124 -> x178, local copies, waits for them, and re-layouts: 70.6 us -> 79.1 us
where the time goes in v1:
time: 733 us; the launch traced here: 721 us
  blocking collectives  286 us (39%)
  local copies, waits for them, and re-layouts  168 us (23%)
  waiting for transfers between devices  91.8 us (13%)
  starting transfers between devices  80.7 us (11%)
  matrix products  55.7 us (8%)
  other arithmetic  28.5 us (4%)
  between operations  10.9 us (1%)
    all_to_all x6, blocking collectives, global_sum(): gathered = lax.all_to_all(spread, ('row', 'col'), 0, 0, tiled=True)  111 us
    unnamed x178, local copies, waits for them, and re-layouts  79.1 us
    all_to_all x4, blocking collectives, precondition(): lax.all_to_all(spectrum, 'row', split_axis=1, concat_axis=2, tiled=True)  54.6 us
    all_to_all x4, blocking collectives, precondition(): lax.all_to_all(spectrum, 'col', split_axis=1, concat_axis=2, tiled=True)  47.1 us
    all_to_all x3, blocking collectives, precondition(): lax.all_to_all(jnp.stack(jnp.split(spectrum, lax.axis_size('row'), axis=2...  38.6 us
    ppermute x14, waiting for transfers between devices, padded(): lax.ppermute(head, axis, [((i + 1) % count, i) for i in range(count)])  37.1 us
    all_to_all x3, blocking collectives, precondition(): lax.all_to_all(spectrum, 'col', split_axis=2, concat_axis=1, tiled=True)  34.4 us
    dot_general x4, matrix products, precondition(): jnp.einsum('kx,cyxz->cyzk', xtable, spectrum.reshape(components, owned_he...  27.1 us
  transfers between devices with their start and end apart: 34, of which 26 were waited for; matrix products, arithmetic and copies ran while one was open for 1% of the time, Pallas kernels for 0%

profile of v1, /device:TPU:30, one launch (start us, length us, event | category | flops | bytes accessed | tf_op | source)
XLA Modules:
  0.0 721.2 jit_solution(16085163063137593767)
XLA Ops:
  103.7 11.7 %all_to_all.260 = f32[3,128,128]{2,0,1:T(4,128)S(1)} all-to-all(f32[3,128,128]{2,0,1:T(4,128)S(1)} %copy.405), channel_id=1, replica_groups=mesh['row'=16,'col'=16] {'col'}, dimensions={1} | all-to-all | bytes 393216 | tf_op jit(solution)/shard_map/all_to_all | solution.py:89
  118.8 13.7 %all_to_all.261 = f32[3,128,128]{2,0,1:T(4,128)S(1)} all-to-all(f32[3,128,128]{2,0,1:T(4,128)S(1)} %copy.410), channel_id=1, replica_groups=mesh['row'=16,'col'=16] {'row'}, dimensions={1} | all-to-all | bytes 393216 | tf_op jit(solution)/shard_map/all_to_all | solution.py:96
  160.5 18.4 %all_to_all.262 = f32[256,1,1]{2,1,0:T(1,128)S(1)} all-to-all(f32[256,1,1]{2,1,0:T(1,128)S(1)} %broadcast_in_dim.23), channel_id=1, replica_groups=mesh['row'=16,'col'=16] {'row','col'}, dimensions={0} | all-to-all | bytes 2048 | tf_op jit(solution)/shard_map/all_to_all | solution.py:36
  180.3 8.9 %all-to-all-start.4 = ((f32[256,1,1]{2,1,0:T(1,128)}), f32[256,1,1]{2,1,0:T(1,128)S(1)}, u32[]{:S(2)}, u32[]{:S(2)}) async-start(f32[256,1,1]{2,1,0:T(1,128)} %broadcast_in_dim.22), calls=%async_computation.4 | async-start | bytes 262144 | tf_op jit(solution)/shard_map/all_to_all | solution.py:36
  190.1 8.8 %all-to-all-done.4 = f32[256,1,1]{2,1,0:T(1,128)S(1)} async-done(((f32[256,1,1]{2,1,0:T(1,128)}), f32[256,1,1]{2,1,0:T(1,128)S(1)}, u32[]{:S(2)}, u32[]{:S(2)}) %all-to-all-start.4) | async-done | bytes 1056 | tf_op jit(solution)/shard_map/all_to_all | solution.py:36
  219.3 13.1 %all_to_all.263 = f32[16,3,8,128]{3,2,1,0:T(8,128)} all-to-all(f32[16,3,8,128]{3,2,1,0:T(8,128)S(1)} %constant_dynamic-update-slice_fusion.16), channel_id=1, replica_groups=mesh['row'=16,'col'=16] {'row'}, dimensions={0} | all-to-all | bytes 393216 | tf_op jit(solution)/shard_map/all_to_all | solution.py:72
  245.9 11.5 %all_to_all.264 = f32[16,1,3072]{2,1,0:T(1,128)S(1)} all-to-all(f32[16,1,3072]{2,1,0:T(1,128)S(1)} %reshape.264), channel_id=1, replica_groups=mesh['row'=16,'col'=16] {'col'}, dimensions={0} | all-to-all | bytes 393216 | tf_op jit(solution)/shard_map/all_to_all | solution.py:81
  267.3 11.8 %all_to_all.265 = f32[3,128,128]{2,0,1:T(4,128)S(1)} all-to-all(f32[3,128,128]{2,0,1:T(4,128)S(1)} %copy.424), channel_id=1, replica_groups=mesh['row'=16,'col'=16] {'col'}, dimensions={1} | all-to-all | bytes 393216 | tf_op jit(solution)/shard_map/all_to_all | solution.py:89
  282.4 13.6 %all_to_all.266 = f32[3,128,128]{2,0,1:T(4,128)S(1)} all-to-all(f32[3,128,128]{2,0,1:T(4,128)S(1)} %copy.429), channel_id=1, replica_groups=mesh['row'=16,'col'=16] {'row'}, dimensions={1} | all-to-all | bytes 393216 | tf_op jit(solution)/shard_map/all_to_all | solution.py:96
  308.2 19.2 %all_to_all.267 = f32[256,1,1]{2,1,0:T(1,128)S(1)} all-to-all(f32[256,1,1]{2,1,0:T(1,128)S(1)} %broadcast_in_dim.24), channel_id=1, replica_groups=mesh['row'=16,'col'=16] {'row','col'}, dimensions={0} | all-to-all | bytes 2048 | tf_op jit(solution)/shard_map/all_to_all | solution.py:36
  348.9 17.9 %all_to_all.268 = f32[256,1,1]{2,1,0:T(1,128)S(1)} all-to-all(f32[256,1,1]{2,1,0:T(1,128)S(1)} %broadcast_in_dim.25), channel_id=1, replica_groups=mesh['row'=16,'col'=16] {'row','col'}, dimensions={0} | all-to-all | bytes 2048 | tf_op jit(solution)/shard_map/all_to_all | solution.py:36
  396.2 12.5 %all_to_all.269 = f32[16,3,8,128]{3,2,1,0:T(8,128)S(1)} all-to-all(f32[16,3,8,128]{3,2,1,0:T(8,128)S(1)} %constant_dynamic-update-slice_fusion.32), channel_id=1, replica_groups=mesh['row'=16,'col'=16] {'row'}, dimensions={0} | all-to-all | bytes 393216 | tf_op jit(solution)/shard_map/all_to_all | solution.py:72
  419.8 11.2 %all_to_all.270 = f32[16,1,3072]{2,1,0:T(1,128)S(1)} all-to-all(f32[16,1,3072]{2,1,0:T(1,128)S(1)} %reshape.266), channel_id=1, replica_groups=mesh['row'=16,'col'=16] {'col'}, dimensions={0} | all-to-all | bytes 393216 | tf_op jit(solution)/shard_map/all_to_all | solution.py:81
  440.9 12.0 %all_to_all.271 = f32[3,128,128]{2,0,1:T(4,128)S(1)} all-to-all(f32[3,128,128]{2,0,1:T(4,128)S(1)} %copy.443), channel_id=1, replica_groups=mesh['row'=16,'col'=16] {'col'}, dimensions={1} | all-to-all | bytes 393216 | tf_op jit(solution)/shard_map/all_to_all | solution.py:89
  456.2 13.7 %all_to_all.272 = f32[3,128,128]{2,0,1:T(4,128)S(1)} all-to-all(f32[3,128,128]{2,0,1:T(4,128)S(1)} %copy.448), channel_id=1, replica_groups=mesh['row'=16,'col'=16] {'row'}, dimensions={1} | all-to-all | bytes 393216 | tf_op jit(solution)/shard_map/all_to_all | solution.py:96
  496.1 18.4 %all_to_all.273 = f32[256,1,1]{2,1,0:T(1,128)S(1)} all-to-all(f32[256,1,1]{2,1,0:T(1,128)S(1)} %broadcast_in_dim.27), channel_id=1, replica_groups=mesh['row'=16,'col'=16] {'row','col'}, dimensions={0} | all-to-all | bytes 2048 | tf_op jit(solution)/shard_map/all_to_all | solution.py:36
  515.8 9.3 %all-to-all-start.16 = ((f32[256,1,1]{2,1,0:T(1,128)}), f32[256,1,1]{2,1,0:T(1,128)S(1)}, u32[]{:S(2)}, u32[]{:S(2)}) async-start(f32[256,1,1]{2,1,0:T(1,128)} %broadcast_in_dim.26), calls=%async_computation.16 | async-start | bytes 262144 | tf_op jit(solution)/shard_map/all_to_all | solution.py:36
  526.0 8.9 %all-to-all-done.16 = f32[256,1,1]{2,1,0:T(1,128)S(1)} async-done(((f32[256,1,1]{2,1,0:T(1,128)}), f32[256,1,1]{2,1,0:T(1,128)S(1)}, u32[]{:S(2)}, u32[]{:S(2)}) %all-to-all-start.16) | async-done | bytes 1056 | tf_op jit(solution)/shard_map/all_to_all | solution.py:36
  555.1 13.1 %all_to_all.274 = f32[16,3,8,128]{3,2,1,0:T(8,128)} all-to-all(f32[16,3,8,128]{3,2,1,0:T(8,128)S(1)} %constant_dynamic-update-slice_fusion.48), channel_id=1, replica_groups=mesh['row'=16,'col'=16] {'row'}, dimensions={0} | all-to-all | bytes 393216 | tf_op jit(solution)/shard_map/all_to_all | solution.py:72
  581.7 11.6 %all_to_all.275 = f32[16,1,3072]{2,1,0:T(1,128)S(1)} all-to-all(f32[16,1,3072]{2,1,0:T(1,128)S(1)} %reshape.268), channel_id=1, replica_groups=mesh['row'=16,'col'=16] {'col'}, dimensions={0} | all-to-all | bytes 393216 | tf_op jit(solution)/shard_map/all_to_all | solution.py:81
  603.2 11.7 %all_to_all.276 = f32[3,128,128]{2,0,1:T(4,128)S(1)} all-to-all(f32[3,128,128]{2,0,1:T(4,128)S(1)} %copy.462), channel_id=1, replica_groups=mesh['row'=16,'col'=16] {'col'}, dimensions={1} | all-to-all | bytes 393216 | tf_op jit(solution)/shard_map/all_to_all | solution.py:89
  618.2 13.6 %all_to_all.277 = f32[3,128,128]{2,0,1:T(4,128)S(1)} all-to-all(f32[3,128,128]{2,0,1:T(4,128)S(1)} %copy.467), channel_id=1, replica_groups=mesh['row'=16,'col'=16] {'row'}, dimensions={1} | all-to-all | bytes 393216 | tf_op jit(solution)/shard_map/all_to_all | solution.py:96
  643.8 19.0 %all_to_all.278 = f32[256,1,1]{2,1,0:T(1,128)S(1)} all-to-all(f32[256,1,1]{2,1,0:T(1,128)S(1)} %broadcast_in_dim.28), channel_id=1, replica_groups=mesh['row'=16,'col'=16] {'row','col'}, dimensions={0} | all-to-all | bytes 2048 | tf_op jit(solution)/shard_map/all_to_all | solution.py:36
  684.2 17.9 %all_to_all.279 = f32[256,1,1]{2,1,0:T(1,128)S(1)} all-to-all(f32[256,1,1]{2,1,0:T(1,128)S(1)} %broadcast_in_dim.29), channel_id=1, replica_groups=mesh['row'=16,'col'=16] {'row','col'}, dimensions={0} | all-to-all | bytes 2048 | tf_op jit(solution)/shard_map/all_to_all | solution.py:36
  (507 shorter events, 388.7 us)
Async XLA Ops:
  1.5 7.0 collective-permute-start
  1.6 7.0 collective-permute-start.1
  10.6 7.4 %collective-permute-start.3 = (f32[5,10,1,256]{3,2,1,0:T(1,128)S(1)}, f32[5,10,1,256]{3,2,1,0:T(1,128)S(1)}, u32[]{:S(2)}, u32[]{:S(2)}) collective-permute-start(f32[5,10,1,256]{3,2,1,0:T(1,128)S(1)} %get-tuple-element.50), channel_id=1, source_target_pairs={{1,0},{2,1},{3,2},{4,3},{5,4},{6,5},{7,6},{8,7},{9,8},{10,9},{11,1... | collective-permute-start | bytes 153608 | tf_op jit(solution)/shard_map/ppermute | solution.py:26
  50.4 16.1 %all-to-all-start = ((f32[16,3,8,128]{3,2,1,0:T(8,128)}), f32[16,3,8,128]{3,2,1,0:T(8,128)S(1)}, u32[]{:S(2)}, u32[]{:S(2)}) async-start(f32[16,3,8,128]{3,2,1,0:T(8,128)} %constant_dynamic-update-slice_fusion), calls=%async_computation | async-start | bytes 393216 | tf_op jit(solution)/shard_map/all_to_all | solution.py:72
  81.3 12.0 %all-to-all-start.1 = ((f32[16,1,3072]{2,1,0:T(1,128)}), f32[16,1,3072]{2,1,0:T(1,128)S(1)}, u32[]{:S(2)}, u32[]{:S(2)}) async-start(f32[16,1,3072]{2,1,0:T(1,128)} %reshape.262), calls=%async_computation.1 | async-start | bytes 393216 | tf_op jit(solution)/shard_map/all_to_all | solution.py:81
  141.5 4.5 collective-permute-start.4
  146.0 5.7 collective-permute-start.6
  150.1 7.4 %collective-permute-start.7 = (f32[3,10,1,256]{3,2,1,0:T(1,128)S(1)}, f32[3,10,1,256]{3,2,1,0:T(1,128)S(1)}, u32[]{:S(2)}, u32[]{:S(2)}) collective-permute-start(f32[3,10,1,256]{3,2,1,0:T(1,128)S(1)} %get-tuple-element.95), channel_id=1, source_target_pairs={{1,0},{2,1},{3,2},{4,3},{5,4},{6,5},{7,6},{8,7},{9,8},{10,9},{11,1... | collective-permute-start | bytes 92168 | tf_op jit(solution)/shard_map/ppermute | solution.py:26
  180.3 18.7 %all-to-all-start.4 = ((f32[256,1,1]{2,1,0:T(1,128)}), f32[256,1,1]{2,1,0:T(1,128)S(1)}, u32[]{:S(2)}, u32[]{:S(2)}) async-start(f32[256,1,1]{2,1,0:T(1,128)} %broadcast_in_dim.22), calls=%async_computation.4 | async-start | bytes 262144 | tf_op jit(solution)/shard_map/all_to_all | solution.py:36
  330.7 4.5 collective-permute-start.8
  335.2 5.4 collective-permute-start.10
  339.0 7.2 %collective-permute-start.11 = (f32[3,10,1,256]{3,2,1,0:T(1,128)S(1)}, f32[3,10,1,256]{3,2,1,0:T(1,128)S(1)}, u32[]{:S(2)}, u32[]{:S(2)}) collective-permute-start(f32[3,10,1,256]{3,2,1,0:T(1,128)S(1)} %get-tuple-element.93), channel_id=1, source_target_pairs={{1,0},{2,1},{3,2},{4,3},{5,4},{6,5},{7,6},{8,7},{9,8},{10,9},{11,1... | collective-permute-start | bytes 92168 | tf_op jit(solution)/shard_map/ppermute | solution.py:26
  369.1 4.5 collective-permute-start.12
  373.6 5.3 collective-permute-start.14
  377.4 7.2 %collective-permute-start.15 = (f32[3,10,1,256]{3,2,1,0:T(1,128)S(1)}, f32[3,10,1,256]{3,2,1,0:T(1,128)S(1)}, u32[]{:S(2)}, u32[]{:S(2)}) collective-permute-start(f32[3,10,1,256]{3,2,1,0:T(1,128)S(1)} %get-tuple-element.91), channel_id=1, source_target_pairs={{1,0},{2,1},{3,2},{4,3},{5,4},{6,5},{7,6},{8,7},{9,8},{10,9},{11,1... | collective-permute-start | bytes 92168 | tf_op jit(solution)/shard_map/ppermute | solution.py:26
  477.3 4.5 collective-permute-start.18
  481.9 5.7 collective-permute-start.20
  486.0 7.2 %collective-permute-start.21 = (f32[3,10,1,256]{3,2,1,0:T(1,128)S(1)}, f32[3,10,1,256]{3,2,1,0:T(1,128)S(1)}, u32[]{:S(2)}, u32[]{:S(2)}) collective-permute-start(f32[3,10,1,256]{3,2,1,0:T(1,128)S(1)} %get-tuple-element.89), channel_id=1, source_target_pairs={{1,0},{2,1},{3,2},{4,3},{5,4},{6,5},{7,6},{8,7},{9,8},{10,9},{11,1... | collective-permute-start | bytes 92168 | tf_op jit(solution)/shard_map/ppermute | solution.py:26
  515.8 19.1 %all-to-all-start.16 = ((f32[256,1,1]{2,1,0:T(1,128)}), f32[256,1,1]{2,1,0:T(1,128)S(1)}, u32[]{:S(2)}, u32[]{:S(2)}) async-start(f32[256,1,1]{2,1,0:T(1,128)} %broadcast_in_dim.26), calls=%async_computation.16 | async-start | bytes 262144 | tf_op jit(solution)/shard_map/all_to_all | solution.py:36
  666.1 4.5 collective-permute-start.22
  670.6 5.4 collective-permute-start.24
  674.4 7.2 %collective-permute-start.25 = (f32[3,10,1,256]{3,2,1,0:T(1,128)S(1)}, f32[3,10,1,256]{3,2,1,0:T(1,128)S(1)}, u32[]{:S(2)}, u32[]{:S(2)}) collective-permute-start(f32[3,10,1,256]{3,2,1,0:T(1,128)S(1)} %get-tuple-element.87), channel_id=1, source_target_pairs={{1,0},{2,1},{3,2},{4,3},{5,4},{6,5},{7,6},{8,7},{9,8},{10,9},{11,1... | collective-permute-start | bytes 92168 | tf_op jit(solution)/shard_map/ppermute | solution.py:26
  708.9 5.3 collective-permute-start.28
  712.7 7.2 %collective-permute-start.29 = (f32[3,10,1,256]{3,2,1,0:T(1,128)S(1)}, f32[3,10,1,256]{3,2,1,0:T(1,128)S(1)}, u32[]{:S(2)}, u32[]{:S(2)}) collective-permute-start(f32[3,10,1,256]{3,2,1,0:T(1,128)S(1)} %get-tuple-element.85), channel_id=1, source_target_pairs={{1,0},{2,1},{3,2},{4,3},{5,4},{6,5},{7,6},{8,7},{9,8},{10,9},{11,1... | collective-permute-start | bytes 92168 | tf_op jit(solution)/shard_map/ppermute | solution.py:26
  (65 other events, 692.3 us)
